TPU v7x, 128 devices: a whole 4x4x4 slice. The times are simulated.
128 devices in a mesh: loop: 16 (over x_hi, z, core), width: 8 (over x_lo, y).
Axes of the slice: x: 4 (x_hi: 2, x_lo: 2; x = x_hi * 2 + x_lo), y: 4, z: 4, core: 2. Of those that a mesh axis runs over, the one named last changes fastest.
Arguments:
- queries: bfloat16 [16384, 4096], P('loop', 'width'), may hold values from -0.0625 to 0.0625
- passages: bfloat16 [16384, 4096], P('loop', 'width'), may hold values from -0.0625 to 0.0625
- teacher: bfloat16 [16384, 4096], P('loop'), may hold values from -5 to 12
- positives: int32 [16384], P('loop'), may hold values from 0 to 4095
Outputs:
- grad_queries: float32 [16384, 4096], P('loop', 'width')
- grad_passages: float32 [16384, 4096], P('loop', 'width')
All inputs are finite; a program needn't handle non-finite values.
Results may differ from a plain program's by a relative error of at most 0.0003.
Values may be sent and summed in bfloat16 or wider, within the bound.
No kernel may reach another device: no remote copies, remote signals or barrier semaphores. Data moves between devices by JAX's collectives and lax.ppermute only.
A program may use at most 192 MiB of HBM per device.

v0:
```python
import jax
import jax.numpy as jnp
from jax import lax
from jax.sharding import PartitionSpec as P

STEPS = 4
SCALE = 20.0


def shifted(block, axis, distance):
    devices = range(lax.axis_size(axis))
    route = [((i - distance) % len(devices), i) for i in devices]
    return lax.ppermute(block, axis, route)


def wide_dot(a, b):
    return jnp.dot(a, b, precision=lax.Precision.HIGH, preferred_element_type=jnp.float32)


def per_device(queries, passages, teacher, positives):
    rows = queries.shape[0]
    width = lax.axis_size("width")
    me = lax.axis_index("width")
    sub = rows // width
    window = STEPS * rows
    q_full = lax.all_gather(queries, "width", axis=1, tiled=True)
    p_cols = lax.all_to_all(passages, "width", 0, 1, tiled=True)
    held_cols = [p_cols]
    held = [passages]
    for step in range(1, STEPS):
        held_cols.append(shifted(held_cols[-1], "loop", 1))
        held.append(shifted(held[-1], "loop", 1))
    cols = jnp.concatenate(held_cols, 0)
    raw = jnp.einsum("qd,cd->qc", q_full, cols, preferred_element_type=jnp.float32)
    gathered = [
        lax.all_gather(raw[:, k * sub : (k + 1) * sub], "width", axis=1, tiled=True)
        for k in range(STEPS)
    ]
    scores = SCALE * raw
    index = positives[:, None]
    column = lax.broadcasted_iota(jnp.int32, teacher.shape, 1)
    t_pos = jnp.sum(jnp.where(column == index, teacher.astype(jnp.float32), 0.0), 1, keepdims=True)
    local = lax.broadcasted_iota(jnp.int32, (1, STEPS * sub), 1)
    wcol = local // sub * rows + me * sub + local % sub
    hit = wcol == index
    teach_cols = (
        lax.dynamic_slice_in_dim(teacher.reshape(rows, STEPS, width, sub), me, 1, 2)
        .reshape(rows, STEPS * sub)
        .astype(jnp.float32)
    )
    pos_part = jnp.sum(jnp.where(hit, scores, 0.0), 1)
    row_part = jnp.sum(scores, 1) - jnp.sum(teach_cols, 1)
    stats = lax.psum(jnp.stack([pos_part, row_part], 0), "width")
    s_pos = stats[0][:, None]
    total = window * (s_pos - t_pos) - stats[1][:, None]
    coef = SCALE * 2.0 / (window - 1)
    block_col = lax.broadcasted_iota(jnp.int32, (rows, rows), 1)
    query_wide = queries.astype(jnp.float32)
    grad_q = None
    terms = []
    for k in range(STEPS):
        block_scores = SCALE * gathered[k]
        errors = (
            s_pos
            - block_scores
            - (t_pos - teacher[:, k * rows : (k + 1) * rows].astype(jnp.float32))
        )
        block_hit = (block_col + k * rows == index).astype(jnp.float32)
        block_slopes = coef * (block_hit * total - errors)
        gq = wide_dot(block_slopes, held[k].astype(jnp.float32))
        grad_q = gq if grad_q is None else grad_q + gq
        terms.append(wide_dot(block_slopes.T, query_wide))
    grad_p = terms[STEPS - 1]
    for k in range(STEPS - 2, -1, -1):
        grad_p = shifted(grad_p, "loop", -1) + terms[k]
    return (grad_q, grad_p)


def solution(mesh):
    in_specs = (P("loop", "width"), P("loop", "width"), P("loop", None), P("loop"))
    out_specs = (P("loop", "width"), P("loop", "width"))
    return jax.shard_map(
        per_device, mesh=mesh, in_specs=in_specs, out_specs=out_specs, check_vma=False
    )
```

profile of v0, /device:TPU:0, one launch (start us, length us, event | category | flops | bytes accessed | tf_op | source)
XLA Modules:
  0.0 438.1 jit_solution(10185207552571837070)
XLA Ops:
  8.0 26.1 %all_to_all.19 = bf16[8,128,512]{2,1,0:T(8,128)(2,1)S(1)} all-to-all(bf16[8,128,512]{2,1,0:T(8,128)(2,1)} %bitcast.24), channel_id=1, replica_groups=mesh['loop'=16,'width'=8] {'width'}, dimensions={0} | all-to-all | bytes 2097152 | tf_op jit(solution)/shard_map/all_to_all | solution.py:27
  34.8 40.4 %collective-permute-done = bf16[128,4096]{0,1:T(8,128)(2,1)S(1)} collective-permute-done((bf16[128,4096]{0,1:T(8,128)(2,1)S(1)}, bf16[128,4096]{0,1:T(8,128)(2,1)S(1)}, u32[]{:S(2)}, u32[]{:S(2)}) %collective-permute-start) | collective-permute-done | bytes 1048608 | tf_op jit(solution)/shard_map/ppermute | solution.py:13
  75.2 40.4 %collective-permute-done.1 = bf16[128,4096]{0,1:T(8,128)(2,1)S(1)} collective-permute-done((bf16[128,4096]{0,1:T(8,128)(2,1)S(1)}, bf16[128,4096]{0,1:T(8,128)(2,1)S(1)}, u32[]{:S(2)}, u32[]{:S(2)}) %collective-permute-start.1) | collective-permute-done | bytes 1048608 | tf_op jit(solution)/shard_map/ppermute | solution.py:13
  115.7 28.3 %collective-permute-done.2 = bf16[128,4096]{0,1:T(8,128)(2,1)} collective-permute-done((bf16[128,4096]{0,1:T(8,128)(2,1)S(1)}, bf16[128,4096]{0,1:T(8,128)(2,1)}, u32[]{:S(2)}, u32[]{:S(2)}) %collective-permute-start.2) | collective-permute-done | bytes 1048608 | tf_op jit(solution)/shard_map/ppermute | solution.py:13
  144.0 8.5 %select_reduce_fusion.1 = (f32[1024]{0:T(1024)S(1)}, f32[1024]{0:T(1024)S(1)}, f32[1024,512]{0,1:T(8,128)S(1)}) fusion(s32[1024]{0:T(1024)S(1)} %copy-done.6, s32[512]{0:T(512)S(1)} %fusion.23, bf16[1024,4096]{1,0:T(8,128)(2,1)} %all-gather.6.cloned.1.call-done, bf16[128,4096]{0,1:T(8,128)(2,1)} %collective-permute-done.2, ...), kind=kOutput, calls=%fused_computation.17 | convolution fusion | flops 4314363904 | bytes 14694400 | tf_op jit(solution)/shard_map/qd,cd->qc/dot_general | solution.py:34
  152.5 1.4 fusion.53
  155.8 9.5 %copy.23 = bf16[128,8,32,128]{3,2,1,0:T(8,128)(2,1)} copy(bf16[128,8,32,128]{3,1,2,0:T(8,128)(2,1)} %bitcast.21) | data formatting | bytes 16777216
  165.3 5.9 %fusion.52 = (bf16[1024,1024]{1,0:T(8,128)(2,1)}, bf16[1024,1024]{1,0:T(8,128)(2,1)}, bf16[1024,1024]{1,0:T(8,128)(2,1)}, bf16[1024,1024]{1,0:T(8,128)(2,1)S(1)}) fusion(bf16[1024,4096]{1,0:T(8,128)(2,1)} %param.6), kind=kLoop, calls=%fused_computation.71 | loop fusion | bytes 16777216 | tf_op jit(solution)/shard_map/slice | solution.py:66
  171.2 4.0 copy.22
  175.1 7.6 %convert_reduce_fusion = f32[1024]{0:T(1024)S(1)} fusion(bf16[1024,4,8,128]{3,2,1,0:T(8,128)(2,1)} %bitcast.22, s32[]{:T(128)S(6)} %select_n.36), kind=kLoop, calls=%fused_computation.16 | loop fusion | flops 1047552 | bytes 1052676 | tf_op jit(solution)/shard_map/reduce_sum | solution.py:52
  182.8 6.4 %select_reduce_fusion = f32[1024]{0:T(1024)S(1)} fusion(bf16[1024,4096]{1,0:T(8,128)(2,1)} %param.6, s32[1024]{0:T(1024)S(1)} %copy-done.6), kind=kLoop, calls=%fused_computation | loop fusion | flops 16776192 | bytes 8396800 | tf_op jit(solution)/shard_map/reduce_sum | solution.py:42
  189.2 20.3 %psum.7 = f32[2,1024]{1,0:T(2,128)S(1)} all-reduce(f32[2,1024]{1,0:T(2,128)S(1)} %pad_maximum_fusion), channel_id=1, replica_groups=mesh['loop'=16,'width'=8] {'width'}, use_global_device_ids=true, to_apply=%region_3.4 | all-reduce | flops 2048 | bytes 16384 | tf_op jit(solution)/shard_map/psum | solution.py:53
  209.6 7.1 %fusion.16 = f32[1024,512]{1,0:T(8,128)} fusion(bf16[1024,512]{1,0:T(8,128)(2,1)S(1)} %copy-done.3, bf16[1024,1024]{0,1:T(8,128)(2,1)} %copy.22, f32[1024,1024]{0,1:T(8,128)} %all-gather.14.cloned.1.call-done, f32[1024]{0:T(1024)S(1)} %select_reduce_fusion, f32[1024]{0:T(1024)S(1)} %bitcast.29, f32[1024]{0:T(1024)S(1)} %multiply_subtract_fusion, ...), kind=kOutput, calls=%fused_computation.26 | convolution fusion | flops 3230662656 | bytes 9457664 | tf_op jit(solution)/shard_map/dot_general | solution.py:17
  217.7 39.7 %collective-permute-done.3 = bf16[1024,512]{1,0:T(8,128)(2,1)} collective-permute-done((bf16[1024,512]{1,0:T(8,128)(2,1)S(1)}, bf16[1024,512]{1,0:T(8,128)(2,1)}, u32[]{:S(2)}, u32[]{:S(2)}) %collective-permute-start.3) | collective-permute-done | bytes 1048608 | tf_op jit(solution)/shard_map/ppermute | solution.py:13
  257.4 3.9 copy.21
  261.3 3.9 copy.20
  265.3 2.5 copy.19
  267.8 8.7 %all-gather.12.cloned.1.call-done = f32[1024,1024]{0,1:T(8,128)} async-done(((f32[1024,128]{0,1:T(8,128)}), f32[1024,1024]{0,1:T(8,128)}) %all-gather.12.cloned.1.call-update) | async-done | bytes 4194320 | tf_op jit(solution)/shard_map/all_gather | solution.py:36
  276.5 7.6 %convolution_add_fusion = f32[1024,512]{1,0:T(8,128)} fusion(f32[1024,512]{1,0:T(8,128)} %collective-permute-done.6, bf16[1024,512]{1,0:T(8,128)(2,1)S(1)} %copy-done.3, bf16[1024,1024]{0,1:T(8,128)(2,1)} %copy.21, f32[1024,1024]{0,1:T(8,128)} %all-gather.12.cloned.1.call-done, f32[1024]{0:T(1024)S(1)} %select_reduce_fusion, f32[1024]{0:T(1024)S(1)} %bitcast.30, ...), kind=kOutput, calls=%fused_computation.20 | convolution fusion | flops 3231186944 | bytes 11554816 | tf_op jit(solution)/shard_map/dot_general | solution.py:17
  284.1 4.0 collective-permute-start.7
  288.3 55.0 %all-gather.8.cloned.1.call-done = f32[1024,1024]{0,1:T(8,128)} async-done(((f32[1024,128]{0,1:T(8,128)}), f32[1024,1024]{0,1:T(8,128)}) %all-gather.8.cloned.1.call-update) | async-done | bytes 4194320 | tf_op jit(solution)/shard_map/all_gather | solution.py:36
  343.3 5.8 %fusion.11 = f32[1024,512]{1,0:T(8,128)S(1)} fusion(bf16[1024,512]{1,0:T(8,128)(2,1)S(1)} %copy-done.3, bf16[1024,1024]{0,1:T(8,128)(2,1)} %copy.19, f32[1024,1024]{0,1:T(8,128)} %all-gather.8.cloned.1.call-done, f32[1024]{0:T(1024)S(1)} %select_reduce_fusion, f32[1024]{0:T(1024)S(1)} %bitcast.31, f32[1024]{0:T(1024)S(1)} %multiply_subtract_fusion, ...), kind=kOutput, calls=%fused_computation.21 | convolution fusion | flops 3230662656 | bytes 9453568 | tf_op jit(solution)/shard_map/dot_general | solution.py:17
  349.1 6.3 %fusion.15 = f32[1024,512]{1,0:T(8,128)} fusion(bf16[1024,512]{1,0:T(8,128)(2,1)} %collective-permute-done.4, bf16[1024,1024]{0,1:T(8,128)(2,1)} %copy.21, f32[1024,1024]{0,1:T(8,128)S(1)} %copy-done.10, f32[1024]{0:T(1024)S(1)} %select_reduce_fusion, f32[1024]{0:T(1024)S(1)} %bitcast.32, f32[1024]{0:T(1024)S(1)} %multiply_subtract_fusion, ...), kind=kOutput, calls=%fused_computation.25 | convolution fusion | flops 3230662656 | bytes 9457664 | tf_op jit(solution)/shard_map/dot_general | solution.py:17
  355.4 38.5 %all-gather.10.cloned.1.call-done = f32[1024,1024]{0,1:T(8,128)} async-done(((f32[1024,128]{0,1:T(8,128)}), f32[1024,1024]{0,1:T(8,128)}) %all-gather.10.cloned.1.call-update) | async-done | bytes 4194320 | tf_op jit(solution)/shard_map/all_gather | solution.py:36
  393.9 5.1 %fusion.13 = f32[1024,512]{1,0:T(8,128)S(1)} fusion(bf16[1024,512]{1,0:T(8,128)(2,1)S(1)} %copy-done.3, bf16[1024,1024]{0,1:T(8,128)(2,1)} %copy.20, f32[1024,1024]{0,1:T(8,128)} %all-gather.10.cloned.1.call-done, f32[1024]{0:T(1024)S(1)} %select_reduce_fusion, f32[1024]{0:T(1024)S(1)} %bitcast.33, f32[1024]{0:T(1024)S(1)} %multiply_subtract_fusion, ...), kind=kOutput, calls=%fused_computation.23 | convolution fusion | flops 3230662656 | bytes 9457664 | tf_op jit(solution)/shard_map/dot_general | solution.py:17
  399.1 2.2 add.95
  401.3 4.6 %collective-permute-start.8 = (f32[1024,512]{1,0:T(8,128)S(1)}, f32[1024,512]{1,0:T(8,128)S(1)}, u32[]{:S(2)}, u32[]{:S(2)}) collective-permute-start(f32[1024,512]{1,0:T(8,128)S(1)} %add.95), channel_id=1, source_target_pairs={{8,0},{16,8},{24,16},{32,24},{40,32},{48,40},{56,48},{64,56},{72,6... | collective-permute-start | bytes 6291464 | tf_op jit(solution)/shard_map/ppermute | solution.py:13
  406.0 3.0 fusion.12
  409.0 4.4 fusion.14
  413.4 5.8 %add_add_fusion = f32[1024,512]{1,0:T(8,128)} fusion(f32[1024,512]{1,0:T(8,128)S(1)} %copy-done.11, f32[1024,512]{1,0:T(8,128)S(1)} %fusion.12, f32[1024,512]{1,0:T(8,128)S(1)} %fusion.14, bf16[1024,512]{1,0:T(8,128)(2,1)} %collective-permute-done.5, bf16[1024,1024]{0,1:T(8,128)(2,1)S(1)} %copy-done, f32[1024,1024]{0,1:T(8,128)S(1)} %copy-done.7, ...), kind=kOutput, calls=%fused_computation.15 | convolution fusion | flops 3232235520 | bytes 15749120 | tf_op jit(solution)/shard_map/dot_general | solution.py:17
  419.2 10.3 %collective-permute-done.8 = f32[1024,512]{1,0:T(8,128)S(1)} collective-permute-done((f32[1024,512]{1,0:T(8,128)S(1)}, f32[1024,512]{1,0:T(8,128)S(1)}, u32[]{:S(2)}, u32[]{:S(2)}) %collective-permute-start.8) | collective-permute-done | bytes 2097184 | tf_op jit(solution)/shard_map/ppermute | solution.py:13
  429.5 1.8 add.96
  (56 shorter events, 4.7 us)
Async XLA Ops:
  7.2 136.8 %copy-start.6 = (s32[1024]{0:T(1024)S(1)}, s32[1024]{0:T(1024)}, u32[]{:S(2)}) copy-start(s32[1024]{0:T(1024)} %param.7) | copy-start | bytes 12292
  7.2 136.8 %all-gather.6.cloned.1.call-start = ((), (), s32[]{:S(2)}) async-start(), calls=%async_computation.1 | async-start | bytes 9437184 | tf_op jit(solution)/shard_map/all_gather | solution.py:26
  7.9 201.7 %all-gather.14.cloned.1.call-start = ((), (), s32[]{:S(2)}) async-start(), calls=%async_computation.5 | async-start | bytes 4718592 | tf_op jit(solution)/shard_map/all_gather | solution.py:36
  34.7 40.5 %collective-permute-start = (bf16[128,4096]{0,1:T(8,128)(2,1)S(1)}, bf16[128,4096]{0,1:T(8,128)(2,1)S(1)}, u32[]{:S(2)}, u32[]{:S(2)}) collective-permute-start(bf16[128,4096]{0,1:T(8,128)(2,1)S(1)} %bitcast.25), channel_id=1, source_target_pairs={{120,0},{0,8},{8,16},{16,24},{24,32},{32,40},{40,48},{48,56},{56,6... | collective-permute-start | bytes 3145736 | tf_op jit(solution)/shard_map/ppermute | solution.py:13
  75.2 40.4 %collective-permute-start.1 = (bf16[128,4096]{0,1:T(8,128)(2,1)S(1)}, bf16[128,4096]{0,1:T(8,128)(2,1)S(1)}, u32[]{:S(2)}, u32[]{:S(2)}) collective-permute-start(bf16[128,4096]{0,1:T(8,128)(2,1)S(1)} %collective-permute-done), channel_id=1, source_target_pairs={{120,0},{0,8},{8,16},{16,24},{24,32},{32,40},{40,48},{48,56},{56,6... | collective-permute-start | bytes 3145736 | tf_op jit(solution)/shard_map/ppermute | solution.py:13
  115.7 28.3 %collective-permute-start.2 = (bf16[128,4096]{0,1:T(8,128)(2,1)S(1)}, bf16[128,4096]{0,1:T(8,128)(2,1)}, u32[]{:S(2)}, u32[]{:S(2)}) collective-permute-start(bf16[128,4096]{0,1:T(8,128)(2,1)S(1)} %collective-permute-done.1), channel_id=1, source_target_pairs={{120,0},{0,8},{8,16},{16,24},{24,32},{32,40},{40,48},{48,56},{56,6... | collective-permute-start | bytes 3145736 | tf_op jit(solution)/shard_map/ppermute | solution.py:13
  153.9 122.6 %all-gather.12.cloned.1.call-start = ((), (), s32[]{:S(2)}) async-start(), calls=%async_computation.4 | async-start | bytes 4718592 | tf_op jit(solution)/shard_map/all_gather | solution.py:36
  154.6 188.6 %all-gather.8.cloned.1.call-start = ((), (), s32[]{:S(2)}) async-start(), calls=%async_computation.2 | async-start | bytes 4718592 | tf_op jit(solution)/shard_map/all_gather | solution.py:36
  155.2 238.7 %all-gather.10.cloned.1.call-start = ((), (), s32[]{:S(2)}) async-start(), calls=%async_computation.3 | async-start | bytes 4718592 | tf_op jit(solution)/shard_map/all_gather | solution.py:36
  182.8 26.8 %copy-start.3 = (bf16[1024,512]{1,0:T(8,128)(2,1)S(1)}, bf16[1024,512]{1,0:T(8,128)(2,1)}, u32[]{:S(2)}) copy-start(bf16[1024,512]{1,0:T(8,128)(2,1)} %param.4) | copy-start | bytes 3145732
  209.6 7.6 %copy-start.4 = (bf16[1024,512]{1,0:T(8,128)(2,1)S(1)}, bf16[1024,512]{1,0:T(8,128)(2,1)}, u32[]{:S(2)}) copy-start(bf16[1024,512]{1,0:T(8,128)(2,1)} %param.5) | copy-start | bytes 3145732
  216.7 59.8 %collective-permute-start.6 = (f32[1024,512]{1,0:T(8,128)}, f32[1024,512]{1,0:T(8,128)}, u32[]{:S(2)}, u32[]{:S(2)}) collective-permute-start(f32[1024,512]{1,0:T(8,128)} %fusion.16), channel_id=1, source_target_pairs={{8,0},{16,8},{24,16},{32,24},{40,32},{48,40},{56,48},{64,56},{72,6... | collective-permute-start | bytes 6291464 | tf_op jit(solution)/shard_map/ppermute | solution.py:13
  217.2 40.2 %collective-permute-start.3 = (bf16[1024,512]{1,0:T(8,128)(2,1)S(1)}, bf16[1024,512]{1,0:T(8,128)(2,1)}, u32[]{:S(2)}, u32[]{:S(2)}) collective-permute-start(bf16[1024,512]{1,0:T(8,128)(2,1)S(1)} %copy-done.4), channel_id=1, source_target_pairs={{120,0},{0,8},{8,16},{16,24},{24,32},{32,40},{40,48},{48,56},{56,6... | collective-permute-start | bytes 3145736 | tf_op jit(solution)/shard_map/ppermute | solution.py:13
  257.4 30.7 %collective-permute-start.4 = (bf16[1024,512]{1,0:T(8,128)(2,1)}, bf16[1024,512]{1,0:T(8,128)(2,1)}, u32[]{:S(2)}, u32[]{:S(2)}) collective-permute-start(bf16[1024,512]{1,0:T(8,128)(2,1)} %collective-permute-done.3), channel_id=1, source_target_pairs={{120,0},{0,8},{8,16},{16,24},{24,32},{32,40},{40,48},{48,56},{56,6... | collective-permute-start | bytes 3145736 | tf_op jit(solution)/shard_map/ppermute | solution.py:13
  284.1 115.0 %collective-permute-start.7 = (f32[1024,512]{1,0:T(8,128)}, f32[1024,512]{1,0:T(8,128)}, u32[]{:S(2)}, u32[]{:S(2)}) collective-permute-start(f32[1024,512]{1,0:T(8,128)} %convolution_add_fusion), channel_id=1, source_target_pairs={{8,0},{16,8},{24,16},{32,24},{40,32},{48,40},{56,48},{64,56},{72,6... | collective-permute-start | bytes 6291464 | tf_op jit(solution)/shard_map/ppermute | solution.py:13
  288.1 125.2 %collective-permute-start.5 = (bf16[1024,512]{1,0:T(8,128)(2,1)}, bf16[1024,512]{1,0:T(8,128)(2,1)}, u32[]{:S(2)}, u32[]{:S(2)}) collective-permute-start(bf16[1024,512]{1,0:T(8,128)(2,1)} %collective-permute-done.4), channel_id=1, source_target_pairs={{120,0},{0,8},{8,16},{16,24},{24,32},{32,40},{40,48},{48,56},{56,6... | collective-permute-start | bytes 3145736 | tf_op jit(solution)/shard_map/ppermute | solution.py:13
  343.3 5.8 %copy-start.10 = (f32[1024,1024]{0,1:T(8,128)S(1)}, f32[1024,1024]{0,1:T(8,128)}, u32[]{:S(2)}) copy-start(f32[1024,1024]{0,1:T(8,128)} %all-gather.12.cloned.1.call-done) | copy-start | bytes 12582916
  393.9 12.1 %copy-start.8 = (f32[1024,1024]{0,1:T(8,128)S(1)}, f32[1024,1024]{0,1:T(8,128)}, u32[]{:S(2)}) copy-start(f32[1024,1024]{0,1:T(8,128)} %all-gather.8.cloned.1.call-done) | copy-start | bytes 12582916
  399.1 6.9 %copy-start.2 = (bf16[1024,1024]{0,1:T(8,128)(2,1)S(1)}, bf16[1024,1024]{0,1:T(8,128)(2,1)}, u32[]{:S(2)}) copy-start(bf16[1024,1024]{0,1:T(8,128)(2,1)} %copy.19) | copy-start | bytes 6291460
  399.1 6.9 %copy-start.5 = (bf16[1024,512]{1,0:T(8,128)(2,1)S(1)}, bf16[1024,512]{1,0:T(8,128)(2,1)}, u32[]{:S(2)}) copy-start(bf16[1024,512]{1,0:T(8,128)(2,1)} %param.5) | copy-start | bytes 3145732
  401.3 7.6 %copy-start.1 = (bf16[1024,1024]{0,1:T(8,128)(2,1)S(1)}, bf16[1024,1024]{0,1:T(8,128)(2,1)}, u32[]{:S(2)}) copy-start(bf16[1024,1024]{0,1:T(8,128)(2,1)} %copy.20) | copy-start | bytes 6291460
  401.3 7.6 %copy-start.9 = (f32[1024,1024]{0,1:T(8,128)S(1)}, f32[1024,1024]{0,1:T(8,128)}, u32[]{:S(2)}) copy-start(f32[1024,1024]{0,1:T(8,128)} %all-gather.10.cloned.1.call-done) | copy-start | bytes 12582916
  401.3 28.2 %collective-permute-start.8 = (f32[1024,512]{1,0:T(8,128)S(1)}, f32[1024,512]{1,0:T(8,128)S(1)}, u32[]{:S(2)}, u32[]{:S(2)}) collective-permute-start(f32[1024,512]{1,0:T(8,128)S(1)} %add.95), channel_id=1, source_target_pairs={{8,0},{16,8},{24,16},{32,24},{40,32},{48,40},{56,48},{64,56},{72,6... | collective-permute-start | bytes 6291464 | tf_op jit(solution)/shard_map/ppermute | solution.py:13
  409.0 4.4 %copy-start = (bf16[1024,1024]{0,1:T(8,128)(2,1)S(1)}, bf16[1024,1024]{0,1:T(8,128)(2,1)}, u32[]{:S(2)}) copy-start(bf16[1024,1024]{0,1:T(8,128)(2,1)} %copy.22) | copy-start | bytes 6291460
  409.0 4.4 %copy-start.7 = (f32[1024,1024]{0,1:T(8,128)S(1)}, f32[1024,1024]{0,1:T(8,128)}, u32[]{:S(2)}) copy-start(f32[1024,1024]{0,1:T(8,128)} %all-gather.14.cloned.1.call-done) | copy-start | bytes 12582916
  409.0 4.4 %copy-start.11 = (f32[1024,512]{1,0:T(8,128)S(1)}, f32[1024,512]{1,0:T(8,128)}, u32[]{:S(2)}) copy-start(f32[1024,512]{1,0:T(8,128)} %fusion.15) | copy-start | bytes 6291460
Sparse Core Ops, SparseCore 0:
  9.6 98.8 all-gather.5
  154.0 50.4 all-gather.13
  206.2 70.2 all-gather.11
  278.0 65.2 all-gather.7
  344.7 49.1 all-gather.9
where the time goes:
time: 444 us; the launch traced here: 438 us
  waiting for transfers between devices  263 us (59%)
  matrix products  53.6 us (12%)
  blocking collectives  46.4 us (10%)
  local copies, waits for them, and re-layouts  31.8 us (7%)
  other arithmetic  18.1 us (4%)
  between operations  14.3 us (3%)
  starting transfers between devices  10.4 us (2%)
    ppermute x9, waiting for transfers between devices, shifted(): return lax.ppermute(block, axis, route)  159 us
    all_gather x4, waiting for transfers between devices, per_device(): lax.all_gather(raw[:, k * sub:(k + 1) * sub], 'width', axis=1, tiled=True)  102 us
    dot_general x8, matrix products, wide_dot(): jnp.dot(a, b, precision=lax.Precision.HIGH, preferred_element_type=jnp.fl...  45.1 us
    all_to_all x1, blocking collectives, per_device(): p_cols = lax.all_to_all(passages, 'width', 0, 1, tiled=True)  26.1 us
    unnamed x29, local copies, waits for them, and re-layouts  23.9 us
    psum x1, blocking collectives, per_device(): stats = lax.psum(jnp.stack([pos_part, row_part], 0), 'width')  20.3 us
    ppermute x9, starting transfers between devices, shifted(): return lax.ppermute(block, axis, route)  9.88 us
  transfers between devices with their start and end apart: 14, of which 8 were waited for; matrix products, arithmetic and copies ran while one was open for 21% of the time, Pallas kernels for 0%

commit v1 on v0

--- a/solution.py
+++ b/solution.py
@@ -33,7 +33,12 @@
     cols = jnp.concatenate(held_cols, 0)
     raw = jnp.einsum("qd,cd->qc", q_full, cols, preferred_element_type=jnp.float32)
     gathered = [
-        lax.all_gather(raw[:, k * sub : (k + 1) * sub], "width", axis=1, tiled=True)
+        jnp.concatenate(
+            lax.all_to_all(
+                jnp.stack([raw[:, k * sub : (k + 1) * sub]] * lax.axis_size("width")), "width", 0, 0
+            ),
+            axis=1,
+        )
         for k in range(STEPS)
     ]
     scores = SCALE * raw

time: 444 us -> 545 us (1.23)
  waiting for transfers between devices: 263 us -> 312 us
  local copies, waits for them, and re-layouts: 31.8 us -> 63.4 us
  matrix products: 53.6 us -> 29.1 us
  other arithmetic: 18.1 us -> 39.9 us
  starting transfers between devices: 10.4 us -> 31.3 us
    all_to_all x0 -> x4, waiting for transfers between devices: none -> 147 us  [per_device(): lax.all_to_all(jnp.stack([raw[:, k * sub:(k + 1) * sub]] * lax.axis_size(...]
    all_gather x4 -> x0, waiting for transfers between devices: 102 us -> none  [per_device(): lax.all_gather(raw[:, k * sub:(k + 1) * sub], 'width', axis=1, tiled=True)]
    dot_general x8, matrix products: 45.1 us -> 20.3 us  [wide_dot(): jnp.dot(a, b, precision=lax.Precision.HIGH, preferred_element_type=jnp.fl...]
    mul x0 -> x5, other arithmetic: none -> 23.8 us  [the longest x4 15.3 us: per_device(): block_scores = SCALE * gathered[k]]
    all_to_all x0 -> x4, local copies, waits for them, and re-layouts: none -> 21.5 us  [per_device(): lax.all_to_all(jnp.stack([raw[:, k * sub:(k + 1) * sub]] * lax.axis_size(...]
    all_to_all x0 -> x4, starting transfers between devices: none -> 19.2 us  [per_device(): lax.all_to_all(jnp.stack([raw[:, k * sub:(k + 1) * sub]] * lax.axis_size(...]
    another operation x0 -> x4, local copies, waits for them, and re-layouts: none -> 8.89 us  [per_device(): jnp.stack([raw[:, k * sub:(k + 1) * sub]] * lax.axis_size('width'))]
    unnamed x29 -> x19, local copies, waits for them, and re-layouts: 23.9 us -> 25.7 us
  transfers between devices with their start and end apart: 14 -> 14, of which waited for: 8 -> 10; matrix products, arithmetic and copies ran while one was open for 21% -> 17% of each run, Pallas kernels for 0% -> 0%
where the time goes in v1:
time: 545 us; the launch traced here: 537 us
  waiting for transfers between devices  312 us (57%)
  local copies, waits for them, and re-layouts  63.4 us (12%)
  blocking collectives  46.5 us (9%)
  other arithmetic  39.9 us (7%)
  starting transfers between devices  31.3 us (6%)
  matrix products  29.1 us (5%)
  between operations  14.5 us (3%)
    ppermute x9, waiting for transfers between devices, shifted(): return lax.ppermute(block, axis, route)  164 us
    all_to_all x4, waiting for transfers between devices, per_device(): lax.all_to_all(jnp.stack([raw[:, k * sub:(k + 1) * sub]] * lax.axis_size(...  147 us
    all_to_all x1, blocking collectives, per_device(): p_cols = lax.all_to_all(passages, 'width', 0, 1, tiled=True)  26.1 us
    unnamed x19, local copies, waits for them, and re-layouts  25.7 us
    all_to_all x4, local copies, waits for them, and re-layouts, per_device(): lax.all_to_all(jnp.stack([raw[:, k * sub:(k + 1) * sub]] * lax.axis_size(...  21.5 us
    psum x1, blocking collectives, per_device(): stats = lax.psum(jnp.stack([pos_part, row_part], 0), 'width')  20.5 us
    dot_general x8, matrix products, wide_dot(): jnp.dot(a, b, precision=lax.Precision.HIGH, preferred_element_type=jnp.fl...  20.3 us
    all_to_all x4, starting transfers between devices, per_device(): lax.all_to_all(jnp.stack([raw[:, k * sub:(k + 1) * sub]] * lax.axis_size(...  19.2 us
  transfers between devices with their start and end apart: 14, of which 10 were waited for; matrix products, arithmetic and copies ran while one was open for 17% of the time, Pallas kernels for 0%

profile of v1, /device:TPU:0, one launch (start us, length us, event | category | flops | bytes accessed | tf_op | source)
XLA Modules:
  0.0 536.5 jit_solution(486693796917809921)
XLA Ops:
  7.9 26.1 %all_to_all.39 = bf16[8,128,512]{2,1,0:T(8,128)(2,1)S(1)} all-to-all(bf16[8,128,512]{2,1,0:T(8,128)(2,1)} %bitcast.72), channel_id=1, replica_groups=mesh['loop'=16,'width'=8] {'width'}, dimensions={0} | all-to-all | bytes 2097152 | tf_op jit(solution)/shard_map/all_to_all | solution.py:27
  34.7 40.4 %collective-permute-done = bf16[128,4096]{0,1:T(8,128)(2,1)S(1)} collective-permute-done((bf16[128,4096]{0,1:T(8,128)(2,1)S(1)}, bf16[128,4096]{0,1:T(8,128)(2,1)S(1)}, u32[]{:S(2)}, u32[]{:S(2)}) %collective-permute-start) | collective-permute-done | bytes 1048608 | tf_op jit(solution)/shard_map/ppermute | solution.py:13
  75.1 40.5 %collective-permute-done.1 = bf16[128,4096]{0,1:T(8,128)(2,1)} collective-permute-done((bf16[128,4096]{0,1:T(8,128)(2,1)S(1)}, bf16[128,4096]{0,1:T(8,128)(2,1)}, u32[]{:S(2)}, u32[]{:S(2)}) %collective-permute-start.1) | collective-permute-done | bytes 1048608 | tf_op jit(solution)/shard_map/ppermute | solution.py:13
  115.7 28.3 %collective-permute-done.2 = bf16[128,4096]{0,1:T(8,128)(2,1)} collective-permute-done((bf16[128,4096]{0,1:T(8,128)(2,1)}, bf16[128,4096]{0,1:T(8,128)(2,1)}, u32[]{:S(2)}, u32[]{:S(2)}) %collective-permute-start.2) | collective-permute-done | bytes 1048608 | tf_op jit(solution)/shard_map/ppermute | solution.py:13
  143.9 8.8 %select_reduce_fusion.1 = (f32[1024]{0:T(1024)S(1)}, f32[1024]{0:T(1024)S(1)}, f32[1024,512]{0,1:T(8,128)S(1)}) fusion(s32[1024]{0:T(1024)S(1)} %copy-done.6, s32[512]{0:T(512)S(1)} %fusion.29, bf16[1024,4096]{1,0:T(8,128)(2,1)} %all-gather.2.cloned.1.call-done, bf16[128,4096]{0,1:T(8,128)(2,1)} %collective-permute-done.2, ...), kind=kOutput, calls=%fused_computation.33 | convolution fusion | flops 4314363904 | bytes 14694400 | tf_op jit(solution)/shard_map/qd,cd->qc/dot_general | solution.py:34
  155.3 5.0 all-to-all-start.4
  160.5 49.1 %all-to-all-done.4 = f32[8,1024,128]{2,1,0:T(8,128)} async-done(((f32[8,1024,128]{2,1,0:T(8,128)}), f32[8,1024,128]{2,1,0:T(8,128)}, u32[]{:S(2)}, u32[]{:S(2)}) %all-to-all-start.4) | async-done | bytes 4194336 | tf_op jit(solution)/shard_map/all_to_all | solution.py:37
  211.8 4.6 all-to-all-start.3
  216.6 49.3 %all-to-all-done.3 = f32[8,1024,128]{2,1,0:T(8,128)} async-done(((f32[8,1024,128]{2,1,0:T(8,128)}), f32[8,1024,128]{2,1,0:T(8,128)}, u32[]{:S(2)}, u32[]{:S(2)}) %all-to-all-start.3) | async-done | bytes 4194336 | tf_op jit(solution)/shard_map/all_to_all | solution.py:37
  268.1 4.6 all-to-all-start.2
  272.9 48.9 %all-to-all-done.2 = f32[8,1024,128]{2,1,0:T(8,128)} async-done(((f32[8,1024,128]{2,1,0:T(8,128)}), f32[8,1024,128]{2,1,0:T(8,128)}, u32[]{:S(2)}, u32[]{:S(2)}) %all-to-all-start.2) | async-done | bytes 4194336 | tf_op jit(solution)/shard_map/all_to_all | solution.py:37
  324.1 5.1 all-to-all-start.1
  329.1 9.5 %copy.41 = bf16[128,8,32,128]{3,2,1,0:T(8,128)(2,1)} copy(bf16[128,8,32,128]{3,1,2,0:T(8,128)(2,1)} %bitcast.69) | data formatting | bytes 16777216
  338.6 5.8 %fusion.34 = (bf16[1024,1024]{1,0:T(8,128)(2,1)S(1)}, bf16[1024,1024]{1,0:T(8,128)(2,1)}, bf16[1024,1024]{1,0:T(8,128)(2,1)}, bf16[1024,1024]{1,0:T(8,128)(2,1)}) fusion(bf16[1024,4096]{1,0:T(8,128)(2,1)} %param.6), kind=kLoop, calls=%fused_computation.57 | loop fusion | bytes 16777216 | tf_op jit(solution)/shard_map/slice | solution.py:71
  344.4 3.9 copy.37
  348.3 4.0 copy.38
  352.2 3.9 copy.39
  358.7 7.6 %convert_reduce_fusion = f32[1024]{0:T(1024)S(1)} fusion(bf16[1024,4,8,128]{3,2,1,0:T(8,128)(2,1)} %bitcast.70, s32[]{:T(128)S(6)} %select_n.36), kind=kLoop, calls=%fused_computation.32 | loop fusion | flops 1047552 | bytes 1052676 | tf_op jit(solution)/shard_map/reduce_sum | solution.py:57
  366.3 6.2 %select_reduce_fusion = f32[1024]{0:T(1024)S(1)} fusion(bf16[1024,4096]{1,0:T(8,128)(2,1)} %param.6, s32[1024]{0:T(1024)S(1)} %copy-done.6), kind=kLoop, calls=%fused_computation | loop fusion | flops 16776192 | bytes 8396800 | tf_op jit(solution)/shard_map/reduce_sum | solution.py:47
  372.5 20.5 %psum.7 = f32[2,1024]{1,0:T(2,128)S(1)} all-reduce(f32[2,1024]{1,0:T(2,128)S(1)} %pad_maximum_fusion), channel_id=1, replica_groups=mesh['loop'=16,'width'=8] {'width'}, use_global_device_ids=true, to_apply=%region_3.4 | all-reduce | flops 2048 | bytes 16384 | tf_op jit(solution)/shard_map/psum | solution.py:58
  393.1 5.4 %copy.35 = f32[8,1024,128]{1,2,0:T(8,128)} copy(f32[8,1024,128]{2,1,0:T(8,128)} %all-to-all-done.4) | data formatting | bytes 8388608 | tf_op jit(solution)/shard_map/all_to_all | solution.py:37
  398.4 5.4 %copy.32 = f32[8,1024,128]{1,2,0:T(8,128)} copy(f32[8,1024,128]{2,1,0:T(8,128)} %all-to-all-done.3) | data formatting | bytes 8388608 | tf_op jit(solution)/shard_map/all_to_all | solution.py:37
  403.8 5.4 %copy.29 = f32[8,1024,128]{1,2,0:T(8,128)} copy(f32[8,1024,128]{2,1,0:T(8,128)} %all-to-all-done.2) | data formatting | bytes 8388608 | tf_op jit(solution)/shard_map/all_to_all | solution.py:37
  409.2 5.1 broadcast_multiply_fusion
  420.4 5.4 copy.26
  425.8 5.2 broadcast_multiply_fusion.3
  431.8 8.4 %fusion.10 = (f32[1024,1024]{0,1:T(8,128)S(1)}, f32[1024,1024]{0,1:T(8,128)S(1)}, f32[1024,1024]{0,1:T(8,128)S(1)}, f32[1024,1024]{0,1:T(8,128)S(1)}) fusion(f32[8,1024,128]{1,2,0:T(8,128)S(1)} %copy-done.3, bf16[1024,1024]{0,1:T(8,128)(2,1)} %copy.40, f32[1024]{0:T(1024)S(1)} %select_reduce_fusion, f32[1024]{0:T(1024)S(1)} %bitcast.76, ...), kind=kLoop, calls=%fused_computation.13 | loop fusion | flops 33554432 | bytes 41971712 | tf_op jit(solution)/shard_map/mul | solution.py:74
  443.2 23.0 %collective-permute-done.6 = f32[1024,512]{1,0:T(8,128)S(1)} collective-permute-done((f32[1024,512]{1,0:T(8,128)S(1)}, f32[1024,512]{1,0:T(8,128)S(1)}, u32[]{:S(2)}, u32[]{:S(2)}) %collective-permute-start.6) | collective-permute-done | bytes 2097184 | tf_op jit(solution)/shard_map/ppermute | solution.py:13
  468.7 5.6 %collective-permute-start.7 = (f32[1024,512]{1,0:T(8,128)S(1)}, f32[1024,512]{1,0:T(8,128)S(1)}, u32[]{:S(2)}, u32[]{:S(2)}) collective-permute-start(f32[1024,512]{1,0:T(8,128)S(1)} %convolution_add_fusion), channel_id=1, source_target_pairs={{8,0},{16,8},{24,16},{32,24},{40,32},{48,40},{56,48},{64,56},{72,6... | collective-permute-start | bytes 6291464 | tf_op jit(solution)/shard_map/ppermute | solution.py:13
  474.2 17.8 %collective-permute-done.4 = bf16[1024,512]{1,0:T(8,128)(2,1)S(1)} collective-permute-done((bf16[1024,512]{1,0:T(8,128)(2,1)S(1)}, bf16[1024,512]{1,0:T(8,128)(2,1)S(1)}, u32[]{:S(2)}, u32[]{:S(2)}) %collective-permute-start.4) | collective-permute-done | bytes 1048608 | tf_op jit(solution)/shard_map/ppermute | solution.py:13
  498.3 5.8 %collective-permute-start.8 = (f32[1024,512]{1,0:T(8,128)S(1)}, f32[1024,512]{1,0:T(8,128)S(1)}, u32[]{:S(2)}, u32[]{:S(2)}) collective-permute-start(f32[1024,512]{1,0:T(8,128)S(1)} %add.95), channel_id=1, source_target_pairs={{8,0},{16,8},{24,16},{32,24},{40,32},{48,40},{56,48},{64,56},{72,6... | collective-permute-start | bytes 6291464 | tf_op jit(solution)/shard_map/ppermute | solution.py:13
  517.4 10.3 %collective-permute-done.8 = f32[1024,512]{1,0:T(8,128)S(1)} collective-permute-done((f32[1024,512]{1,0:T(8,128)S(1)}, f32[1024,512]{1,0:T(8,128)S(1)}, u32[]{:S(2)}, u32[]{:S(2)}) %collective-permute-start.8) | collective-permute-done | bytes 2097184 | tf_op jit(solution)/shard_map/ppermute | solution.py:13
  (58 shorter events, 47.3 us)
Async XLA Ops:
  7.2 136.8 %copy-start.6 = (s32[1024]{0:T(1024)S(1)}, s32[1024]{0:T(1024)}, u32[]{:S(2)}) copy-start(s32[1024]{0:T(1024)} %param.7) | copy-start | bytes 12292
  7.2 136.8 %all-gather.2.cloned.1.call-start = ((), (), s32[]{:S(2)}) async-start(), calls=%async_computation.5 | async-start | bytes 9437184 | tf_op jit(solution)/shard_map/all_gather | solution.py:26
  34.6 40.5 %collective-permute-start = (bf16[128,4096]{0,1:T(8,128)(2,1)S(1)}, bf16[128,4096]{0,1:T(8,128)(2,1)S(1)}, u32[]{:S(2)}, u32[]{:S(2)}) collective-permute-start(bf16[128,4096]{0,1:T(8,128)(2,1)S(1)} %bitcast.73), channel_id=1, source_target_pairs={{120,0},{0,8},{8,16},{16,24},{24,32},{32,40},{40,48},{48,56},{56,6... | collective-permute-start | bytes 3145736 | tf_op jit(solution)/shard_map/ppermute | solution.py:13
  75.1 40.5 %collective-permute-start.1 = (bf16[128,4096]{0,1:T(8,128)(2,1)S(1)}, bf16[128,4096]{0,1:T(8,128)(2,1)}, u32[]{:S(2)}, u32[]{:S(2)}) collective-permute-start(bf16[128,4096]{0,1:T(8,128)(2,1)S(1)} %collective-permute-done), channel_id=1, source_target_pairs={{120,0},{0,8},{8,16},{16,24},{24,32},{32,40},{40,48},{48,56},{56,6... | collective-permute-start | bytes 3145736 | tf_op jit(solution)/shard_map/ppermute | solution.py:13
  115.7 28.3 %collective-permute-start.2 = (bf16[128,4096]{0,1:T(8,128)(2,1)}, bf16[128,4096]{0,1:T(8,128)(2,1)}, u32[]{:S(2)}, u32[]{:S(2)}) collective-permute-start(bf16[128,4096]{0,1:T(8,128)(2,1)} %collective-permute-done.1), channel_id=1, source_target_pairs={{120,0},{0,8},{8,16},{16,24},{24,32},{32,40},{40,48},{48,56},{56,6... | collective-permute-start | bytes 3145736 | tf_op jit(solution)/shard_map/ppermute | solution.py:13
  155.3 54.3 %all-to-all-start.4 = ((f32[8,1024,128]{2,1,0:T(8,128)}), f32[8,1024,128]{2,1,0:T(8,128)}, u32[]{:S(2)}, u32[]{:S(2)}) async-start(f32[8,1024,128]{2,1,0:T(8,128)} %stack.17), calls=%async_computation.4 | async-start | bytes 8388608 | tf_op jit(solution)/shard_map/all_to_all | solution.py:37
  211.8 54.1 %all-to-all-start.3 = ((f32[8,1024,128]{2,1,0:T(8,128)}), f32[8,1024,128]{2,1,0:T(8,128)}, u32[]{:S(2)}, u32[]{:S(2)}) async-start(f32[8,1024,128]{2,1,0:T(8,128)} %stack.16), calls=%async_computation.3 | async-start | bytes 8388608 | tf_op jit(solution)/shard_map/all_to_all | solution.py:37
  268.1 53.7 %all-to-all-start.2 = ((f32[8,1024,128]{2,1,0:T(8,128)}), f32[8,1024,128]{2,1,0:T(8,128)}, u32[]{:S(2)}, u32[]{:S(2)}) async-start(f32[8,1024,128]{2,1,0:T(8,128)} %stack.15), calls=%async_computation.2 | async-start | bytes 8388608 | tf_op jit(solution)/shard_map/all_to_all | solution.py:37
  324.1 96.4 %all-to-all-start.1 = ((f32[8,1024,128]{2,1,0:T(8,128)}), f32[8,1024,128]{2,1,0:T(8,128)}, u32[]{:S(2)}, u32[]{:S(2)}) async-start(f32[8,1024,128]{2,1,0:T(8,128)} %stack.14), calls=%async_computation.1 | async-start | bytes 8388608 | tf_op jit(solution)/shard_map/all_to_all | solution.py:37
  409.2 5.1 copy-start.1
  414.3 3.7 copy-start.2
  425.8 5.2 copy-start.3
  425.8 6.0 %copy-start.4 = (f32[8,1024,128]{1,2,0:T(8,128)S(1)}, f32[8,1024,128]{1,2,0:T(8,128)}, u32[]{:S(2)}) copy-start(f32[8,1024,128]{1,2,0:T(8,128)} %broadcast_multiply_fusion.1) | copy-start | bytes 12582916
  431.8 8.5 %copy-start = (bf16[1024,512]{1,0:T(8,128)(2,1)S(1)}, bf16[1024,512]{1,0:T(8,128)(2,1)}, u32[]{:S(2)}) copy-start(bf16[1024,512]{1,0:T(8,128)(2,1)} %param.4) | copy-start | bytes 3145732
  440.3 2.5 copy-start.5
  442.7 23.6 %collective-permute-start.6 = (f32[1024,512]{1,0:T(8,128)S(1)}, f32[1024,512]{1,0:T(8,128)S(1)}, u32[]{:S(2)}, u32[]{:S(2)}) collective-permute-start(f32[1024,512]{1,0:T(8,128)S(1)} %fusion.40), channel_id=1, source_target_pairs={{8,0},{16,8},{24,16},{32,24},{40,32},{48,40},{56,48},{64,56},{72,6... | collective-permute-start | bytes 6291464 | tf_op jit(solution)/shard_map/ppermute | solution.py:13
  442.7 31.5 %collective-permute-start.3 = (bf16[1024,512]{1,0:T(8,128)(2,1)S(1)}, bf16[1024,512]{1,0:T(8,128)(2,1)S(1)}, u32[]{:S(2)}, u32[]{:S(2)}) collective-permute-start(bf16[1024,512]{1,0:T(8,128)(2,1)S(1)} %copy-done.5), channel_id=1, source_target_pairs={{120,0},{0,8},{8,16},{16,24},{24,32},{32,40},{40,48},{48,56},{56,6... | collective-permute-start | bytes 3145736 | tf_op jit(solution)/shard_map/ppermute | solution.py:13
  468.7 29.1 %collective-permute-start.7 = (f32[1024,512]{1,0:T(8,128)S(1)}, f32[1024,512]{1,0:T(8,128)S(1)}, u32[]{:S(2)}, u32[]{:S(2)}) collective-permute-start(f32[1024,512]{1,0:T(8,128)S(1)} %convolution_add_fusion), channel_id=1, source_target_pairs={{8,0},{16,8},{24,16},{32,24},{40,32},{48,40},{56,48},{64,56},{72,6... | collective-permute-start | bytes 6291464 | tf_op jit(solution)/shard_map/ppermute | solution.py:13
  474.2 17.8 %collective-permute-start.4 = (bf16[1024,512]{1,0:T(8,128)(2,1)S(1)}, bf16[1024,512]{1,0:T(8,128)(2,1)S(1)}, u32[]{:S(2)}, u32[]{:S(2)}) collective-permute-start(bf16[1024,512]{1,0:T(8,128)(2,1)S(1)} %collective-permute-done.3), channel_id=1, source_target_pairs={{120,0},{0,8},{8,16},{16,24},{24,32},{32,40},{40,48},{48,56},{56,6... | collective-permute-start | bytes 3145736 | tf_op jit(solution)/shard_map/ppermute | solution.py:13
  492.1 21.5 %collective-permute-start.5 = (bf16[1024,512]{1,0:T(8,128)(2,1)S(1)}, bf16[1024,512]{1,0:T(8,128)(2,1)S(1)}, u32[]{:S(2)}, u32[]{:S(2)}) collective-permute-start(bf16[1024,512]{1,0:T(8,128)(2,1)S(1)} %collective-permute-done.4), channel_id=1, source_target_pairs={{120,0},{0,8},{8,16},{16,24},{24,32},{32,40},{40,48},{48,56},{56,6... | collective-permute-start | bytes 3145736 | tf_op jit(solution)/shard_map/ppermute | solution.py:13
  498.3 29.4 %collective-permute-start.8 = (f32[1024,512]{1,0:T(8,128)S(1)}, f32[1024,512]{1,0:T(8,128)S(1)}, u32[]{:S(2)}, u32[]{:S(2)}) collective-permute-start(f32[1024,512]{1,0:T(8,128)S(1)} %add.95), channel_id=1, source_target_pairs={{8,0},{16,8},{24,16},{32,24},{40,32},{48,40},{56,48},{64,56},{72,6... | collective-permute-start | bytes 6291464 | tf_op jit(solution)/shard_map/ppermute | solution.py:13
Sparse Core Ops, SparseCore 0:
  9.6 98.7 all-gather.1
